TPU v7x, 256 devices: a whole 4x4x8 slice. The times are simulated.
256 devices in a mesh: row: 4 (over y), col: 4 (over x), dp: 16 (over z, core).
Axes of the slice: x: 4, y: 4, z: 8, core: 2. Of those that a mesh axis runs over, the one named last changes fastest.
Arguments:
- hidden_states: bfloat16 [16384, 1536], P(('dp', 'row'), 'col'), may hold values from -18 to 18
- w_query: bfloat16 [1536, 1536], P('col', 'row'), may hold values from -0.102062073 to 0.102062073
- w_key_value: bfloat16 [1536, 512], P('col'), may hold values from -0.102062073 to 0.102062073
- adapter_down: bfloat16 [1024, 1536, 16], P('dp', 'col'), may hold values from -0.15625 to 0.15625
- adapter_up: bfloat16 [1024, 16, 1536], P('dp', None, 'row'), may hold values from -1.5 to 1.5
- req_lengths: int32 [16, 8], replicated, may hold values from 1 to 160, 960 in all within a row
- req_adapter: int32 [16, 8], replicated, may hold values from 0 to 1023, as said below
Outputs:
- attention: bfloat16 [16384, 1536], P(('dp', 'col'), 'row')
- kv_cache: bfloat16 [16384, 512], P(('dp', 'col'))
Inputs may be any that keep to these rules, and one draw needn't show every extreme that they name: `req_lengths`: the lengths of one block sum to 960, and each block has a request of exactly 160 tokens. `req_adapter`: adapters k * 64 to (k + 1) * 64 - 1 are those of index k of dp; the requests of one block use adapters of one index of dp at most 1 times, and some index of dp is used exactly that often by every block.
All inputs are finite; a program needn't handle non-finite values.
Results may differ from a plain program's by a relative error of at most 0.0072.
Values may be sent and summed in bfloat16 or wider, within the bound.
No kernel may reach another device: no remote copies, remote signals or barrier semaphores. Data moves between devices by JAX's collectives and lax.ppermute only.
A program may use at most 128 MiB of HBM per device.

v0:
```python
import math
import jax
import jax.numpy as jnp
from jax import lax
from jax.sharding import PartitionSpec as P

HEAD_DIM = 128
MOST_LEN = 160
masked_score = -1e30


def block_layout(lengths_row, block_len):
    prefix_len = block_len - jnp.sum(lengths_row)
    ends_at = jnp.cumsum(lengths_row) + prefix_len
    starts = ends_at - lengths_row
    positions = jnp.arange(block_len, dtype=jnp.int32)
    segment = jnp.sum((positions[:, None] >= starts[None, :]).astype(jnp.int32), axis=1)
    return (starts, segment, positions)


def slot_numbers(holders):
    request_total = holders.shape[0]
    ordering = jnp.arange(request_total, dtype=jnp.int32)
    earlier = ordering[None, :] < ordering[:, None]
    same_holder = holders[:, None] == holders[None, :]
    return jnp.sum((earlier & same_holder).astype(jnp.int32), axis=1)


def make_attend(query_rows, segment, first_row, kv_group, head_size, kv_half):
    own_rows = query_rows.shape[0]
    heads_here = query_rows.shape[1] // head_size
    query_heads = query_rows.reshape(own_rows, heads_here, head_size)
    query_pos = first_row + jnp.arange(own_rows, dtype=jnp.int32)
    query_seg = lax.dynamic_slice_in_dim(segment, first_row, own_rows, 0)
    score_scale = 1.0 / math.sqrt(head_size)

    def attend(state_in, key_block, key_start):
        running_max, running_sum, running_out = state_in
        block_size = key_block.shape[0]
        key_rows = lax.dynamic_slice_in_dim(key_block, kv_group * head_size, head_size, 1)
        values = lax.dynamic_slice_in_dim(key_block, kv_half + kv_group * head_size, head_size, 1)
        key_pos = jnp.arange(block_size, dtype=jnp.int32)
        allowed = (key_pos[None, :] <= query_pos[:, None]) & (
            (segment[None, :] == query_seg[:, None]) | (segment[None, :] == 0)
        )
        scores = (
            jnp.einsum("qhd,kd->hqk", query_heads, key_rows, preferred_element_type=jnp.float32)
            * score_scale
        )
        scores = jnp.where(allowed[None], scores, masked_score)
        new_max = jnp.maximum(running_max, jnp.max(scores, axis=2))
        weights = jnp.where(allowed[None], jnp.exp(scores - new_max[:, :, None]), 0.0)
        running_sum = jnp.sum(weights, axis=2)
        running_out = jnp.einsum(
            "hqk,kd->hqd", weights.astype(jnp.bfloat16), values, preferred_element_type=jnp.float32
        )
        return (new_max, running_sum, running_out)

    initial = (
        jnp.full((heads_here, own_rows), masked_score, jnp.float32),
        jnp.zeros((heads_here, own_rows), jnp.float32),
        jnp.zeros((heads_here, own_rows, head_size), jnp.float32),
    )
    return (attend, initial)


def body(hidden_states, w_query, w_key_value, adapter_down, adapter_up, req_lengths, req_adapter):
    dp_size = lax.axis_size("dp")
    block_index = lax.axis_index("dp")
    col_index = lax.axis_index("col")
    row_index = lax.axis_index("row")
    gathered = lax.all_gather(hidden_states, "row", axis=0, tiled=True)
    block_len = gathered.shape[0]
    query_cols = w_query.shape[1]
    kv_cols = w_key_value.shape[1]
    kv_half = kv_cols // 2
    head_size = HEAD_DIM
    heads_here = query_cols // head_size
    heads_total = heads_here * lax.axis_size("row")
    kv_heads = kv_half // head_size
    kv_group = row_index * heads_here // (heads_total // kv_heads)
    own_rows = block_len // lax.axis_size("col")
    first_row = col_index * own_rows
    held_sets = adapter_down.shape[0]
    width_here = adapter_down.shape[1]
    rank_size = adapter_down.shape[2]
    lengths_row = req_lengths[block_index]
    adapters_row = req_adapter[block_index]
    requests = lengths_row.shape[0]
    starts, segment, positions = block_layout(lengths_row, block_len)
    request_of = jnp.clip(segment - 1, 0, requests - 1)
    in_request = segment > 0
    holders = adapters_row // held_sets
    slot_of = slot_numbers(holders)
    per_holder = (requests + dp_size - 1) // dp_size
    longest = MOST_LEN
    target_ids = jnp.arange(dp_size, dtype=jnp.int32)[:, None, None]
    slot_ids = jnp.arange(per_holder, dtype=jnp.int32)[None, :, None]
    pairing = (holders[None, None, :] == target_ids) & (slot_of[None, None, :] == slot_ids)
    pair_int = pairing.astype(jnp.int32)
    slot_start = jnp.sum(pair_int * starts[None, None, :], axis=2)
    slot_len = jnp.sum(pair_int * lengths_row[None, None, :], axis=2)
    slot_adapter = jnp.where(
        jnp.any(pairing, axis=2),
        jnp.sum(pair_int * (adapters_row % held_sets)[None, None, :], axis=2),
        -1,
    )
    offsets = jnp.arange(longest, dtype=jnp.int32)
    token_at = slot_start[:, :, None] + offsets[None, None, :]
    live_rows = offsets[None, None, :] < slot_len[:, :, None]
    outgoing = jnp.where(
        live_rows[..., None],
        gathered[jnp.clip(token_at, 0, block_len - 1)],
        jnp.zeros((), gathered.dtype),
    )
    flat_down = jnp.transpose(adapter_down, (1, 0, 2)).reshape(width_here, held_sets * rank_size)
    flat_up = adapter_up.reshape(held_sets * rank_size, query_cols).astype(jnp.float32)
    rank_owner = jnp.arange(held_sets * rank_size, dtype=jnp.int32) // rank_size
    sent_rows = lax.all_to_all(outgoing, "dp", split_axis=0, concat_axis=0, tiled=True)
    sent_ids = lax.all_to_all(
        slot_adapter.astype(jnp.bfloat16), "dp", split_axis=0, concat_axis=0, tiled=True
    )
    reduced = jnp.einsum("nkld,da->nkla", sent_rows, flat_down, preferred_element_type=jnp.float32)
    kept_cols = rank_owner[None, None, :] == sent_ids.astype(jnp.int32)[:, :, None]
    reduced = jnp.where(kept_cols[:, :, None, :], reduced, 0.0)
    adapter_part = jnp.einsum("nkla,af->nklf", reduced, flat_up, precision=lax.Precision.HIGHEST)
    returned = lax.all_to_all(adapter_part, "dp", split_axis=0, concat_axis=0, tiled=True)
    flat_index = (holders[request_of] * per_holder + slot_of[request_of]) * longest + jnp.clip(
        positions - starts[request_of], 0, longest - 1
    )
    adapter_term = returned.reshape(-1, query_cols)[flat_index]
    adapter_term = jnp.where(in_request[:, None], adapter_term, 0.0)
    both_weights = jnp.concatenate([w_query, w_key_value], axis=1)
    partial_value = jnp.dot(gathered, both_weights, preferred_element_type=jnp.float32)
    summed = lax.psum_scatter(
        partial_value
        + jnp.concatenate(
            [adapter_term, jnp.zeros((own_rows * lax.axis_size("col"), kv_cols), jnp.float32)],
            axis=1,
        ),
        "col",
        scatter_dimension=0,
        tiled=True,
    )
    query_rows = summed[:, :query_cols].astype(jnp.bfloat16)
    kv_cache = summed[:, query_cols:].astype(jnp.bfloat16)
    attend, initial = make_attend(query_rows, segment, first_row, kv_group, head_size, kv_half)
    running_max, running_sum, running_out = attend(
        initial, lax.all_gather(kv_cache, "col", axis=0, tiled=True), jnp.int32(0)
    )
    attention = (running_out / running_sum[:, :, None]).astype(jnp.bfloat16)
    attention = jnp.transpose(attention, (1, 0, 2)).reshape(own_rows, query_cols)
    return (attention, kv_cache)


def solution(mesh):
    return jax.shard_map(
        body,
        mesh=mesh,
        in_specs=(
            P(("dp", "row"), "col"),
            P("col", "row"),
            P("col", None),
            P("dp", "col", None),
            P("dp", None, "row"),
            P(),
            P(),
        ),
        out_specs=(P(("dp", "col"), "row"), P(("dp", "col"), None)),
        check_vma=False,
    )
```

profile of v0, /device:TPU:8, one launch (start us, length us, event | category | flops | bytes accessed | tf_op | source)
XLA Modules:
  0.0 303.4 jit_solution(6985747026854632109)
XLA Ops:
  7.2 1.5 fusion.34
  11.0 0.7 copy.46
  11.7 8.6 %all-to-all-start = ((bf16[16,1,1]{2,1,0:T(2,128)(2,1)}), bf16[16,1,1]{2,1,0:T(2,128)(2,1)}, u32[]{:S(2)}, u32[]{:S(2)}) async-start(bf16[16,1,1]{2,1,0:T(2,128)(2,1)} %copy.46), calls=%async_computation | async-start | bytes 16384 | tf_op jit(solution)/shard_map/all_to_all | solution.py:120
  20.5 14.9 %all_gather.6 = bf16[1024,384]{1,0:T(8,128)(2,1)S(1)} all-gather(bf16[256,384]{1,0:T(8,128)(2,1)} %param.7), channel_id=1, replica_groups=mesh['row'=4,'col'=4,'dp'=16] {'row'}, dimensions={0}, use_global_device_ids=true | all-gather | bytes 983040 | tf_op jit(solution)/shard_map/all_gather | solution.py:72
  35.5 7.5 %gather_fusion = bf16[2560,384]{1,0:T(8,128)(2,1)S(1)} fusion(bf16[1024,384]{1,0:T(8,128)(2,1)S(1)} %all_gather.6, s32[3072]{0:T(1024)S(1)} %pad_clamp_fusion), kind=kCustom, calls=%fused_computation | custom fusion | bytes 3942400 | tf_op jit(solution)/shard_map/gather | solution.py:113
  43.0 1.5 broadcast_select_fusion
  44.5 7.0 %all-to-all-start.1 = ((bf16[16,1,160,384]{3,2,1,0:T(8,128)(2,1)}), bf16[16,1,160,384]{3,2,1,0:T(8,128)(2,1)S(1)}, u32[]{:S(2)}, u32[]{:S(2)}) async-start(bf16[16,1,160,384]{3,2,1,0:T(8,128)(2,1)} %broadcast_select_fusion), calls=%async_computation.1 | async-start | bytes 3932160 | tf_op jit(solution)/shard_map/all_to_all | solution.py:119
  51.5 1.1 convert_reduce_fusion.1
  52.7 45.2 %all-to-all-done.1 = bf16[16,1,160,384]{3,2,1,0:T(8,128)(2,1)S(1)} async-done(((bf16[16,1,160,384]{3,2,1,0:T(8,128)(2,1)}), bf16[16,1,160,384]{3,2,1,0:T(8,128)(2,1)S(1)}, u32[]{:S(2)}, u32[]{:S(2)}) %all-to-all-start.1) | async-done | bytes 1966112 | tf_op jit(solution)/shard_map/all_to_all | solution.py:119
  97.9 3.0 fusion.10
  100.9 10.3 %fusion.7 = f32[16,1,160,384]{3,2,1,0:T(8,128)} fusion(bf16[1024,384,1]{1,0,2:T(8,128)(2,1)S(1)} %bitcast.109, f32[16,160,1024]{2,1,0:T(8,128)S(1)} %fusion.10, pred[16,1024]{1,0:T(8,128)(4,1)S(1)} %broadcast_compare_fusion), kind=kOutput, calls=%fused_computation.12 | convolution fusion | flops 12082216960 | bytes 15220736 | tf_op jit(solution)/shard_map/nkla,af->nklf/dot_general | solution.py:126
  111.2 4.8 %all-to-all-start.2 = ((f32[16,1,160,384]{3,2,1,0:T(8,128)}), f32[16,1,160,384]{3,2,1,0:T(8,128)}, u32[]{:S(2)}, u32[]{:S(2)}) async-start(f32[16,1,160,384]{3,2,1,0:T(8,128)} %fusion.7), calls=%async_computation.2 | async-start | bytes 7864320 | tf_op jit(solution)/shard_map/all_to_all | solution.py:127
  116.2 0.7 fusion.52
  117.6 0.7 fusion.53
  118.4 4.1 %select_select_fusion.2 = s32[1024,1]{0,1:T(1,128)S(1)} fusion(s32[]{:T(128)} %bitcast.20, s32[]{:T(128)} %bitcast.21, s32[]{:T(128)} %bitcast.22, s32[]{:T(128)} %bitcast.23, s32[]{:T(128)} %bitcast.24, s32[]{:T(128)} %bitcast.26, s32[]{:T(128)} %bitcast.25, s32[1024,1]{0,1:T(1,128)S(1)} %bitcast.113), kind=kLoop, calls=%fused_computation.56 | loop fusion | flops 15360 | bytes 8220 | tf_op jit(solution)/shard_map/gather | solution.py:128
  122.5 9.0 %select_select_fusion = (s32[1024,1]{0,1:T(1,128)S(1)}, s32[1024,1]{0,1:T(1,128)S(1)}) fusion(s32[]{:T(128)} %bitcast.39, s32[]{:T(128)} %bitcast.40, s32[]{:T(128)} %bitcast.41, s32[]{:T(128)} %bitcast.42, s32[]{:T(128)} %bitcast.43, s32[]{:T(128)} %bitcast.45, s32[]{:T(128)} %bitcast.44, s32[1024,1]{0,1:T(1,128)S(1)} %bitcast.114, s32[]{:T(128)} %bitcast.35, ...), kind=kLoop, calls=%fused_computation.54 | loop fusion | flops 21504 | bytes 12344 | tf_op jit(solution)/shard_map/gather | solution.py:129
  131.6 1.9 broadcast_select_fusion.2
  133.5 71.2 %all-to-all-done.2 = f32[16,1,160,384]{3,2,1,0:T(8,128)} async-done(((f32[16,1,160,384]{3,2,1,0:T(8,128)}), f32[16,1,160,384]{3,2,1,0:T(8,128)}, u32[]{:S(2)}, u32[]{:S(2)}) %all-to-all-start.2) | async-done | bytes 3932192 | tf_op jit(solution)/shard_map/all_to_all | solution.py:127
  204.7 7.1 %gather_fusion.1 = f32[1024,384]{1,0:T(8,128)} fusion(f32[2560,384]{1,0:T(8,128)} %bitcast.17, s32[1024]{0:T(1024)S(1)} %broadcast_clamp_fusion), kind=kCustom, calls=%fused_computation.1 | custom fusion | bytes 3149824 | tf_op jit(solution)/shard_map/gather | solution.py:131
  211.8 1.9 copy.50
  213.9 0.8 copy-done.3
  214.7 3.0 bitcast_add_fusion
  217.8 43.7 %reduce-scatter.2.cloned.1.call-done = f32[256,896]{0,1:T(8,128)} async-done(((f32[1024,896]{0,1:T(8,128)}), f32[256,896]{0,1:T(8,128)}) %reduce-scatter.2.cloned.1.call-update) | async-done | bytes 917520 | tf_op jit(solution)/shard_map/reduce_scatter | solution.py:135
  261.5 1.2 convert.5
  262.7 0.7 slice.41
  263.6 0.8 fusion.18
  264.4 1.8 copy.55
  266.2 25.1 %all-gather.2.cloned.1.call-done = bf16[1024,512]{0,1:T(8,128)(2,1)} async-done(((bf16[256,512]{0,1:T(8,128)(2,1)}), bf16[1024,512]{0,1:T(8,128)(2,1)}) %all-gather.2.cloned.1.call-update) | async-done | bytes 1048592 | tf_op jit(solution)/shard_map/all_gather | solution.py:149
  291.3 1.7 fusion.4
  293.0 0.8 fusion.5
  293.8 1.9 fusion.22
  295.8 0.8 copy.54
  (60 shorter events, 3.4 us)
Async XLA Ops:
  7.2 90.7 %copy-start = (bf16[64,384,16]{1,2,0:T(8,128)(2,1)S(1)}, bf16[64,384,16]{1,2,0:T(8,128)(2,1)}, u32[]{:S(2)}) copy-start(bf16[64,384,16]{1,2,0:T(8,128)(2,1)} %param.10) | copy-start | bytes 2359300
  8.8 11.6 %copy-start.10 = (s32[1,8]{1,0:T(1,128)}, s32[1,8]{1,0:T(1,128)S(1)}, u32[]{:S(2)}) copy-start(s32[1,8]{1,0:T(1,128)S(1)} %copy.62) | copy-start | bytes 100
  8.9 11.4 %copy-start.12 = (s32[8,1]{0,1:T(1,128)}, s32[8,1]{0,1:T(1,128)S(1)}, u32[]{:S(2)}) copy-start(s32[8,1]{0,1:T(1,128)S(1)} %reduce-window.4) | copy-start | bytes 100
  9.0 11.4 %copy-start.6 = (s32[8]{0:T(128)}, s32[8]{0:T(128)S(1)}, u32[]{:S(2)}) copy-start(s32[8]{0:T(128)S(1)} %get-tuple-element.49) | copy-start | bytes 100
  9.1 0.5 copy-start.8
  10.4 0.5 copy-start.4
  11.7 32.8 %all-to-all-start = ((bf16[16,1,1]{2,1,0:T(2,128)(2,1)}), bf16[16,1,1]{2,1,0:T(2,128)(2,1)}, u32[]{:S(2)}, u32[]{:S(2)}) async-start(bf16[16,1,1]{2,1,0:T(2,128)(2,1)} %copy.46), calls=%async_computation | async-start | bytes 16384 | tf_op jit(solution)/shard_map/all_to_all | solution.py:120
  44.5 53.4 %all-to-all-start.1 = ((bf16[16,1,160,384]{3,2,1,0:T(8,128)(2,1)}), bf16[16,1,160,384]{3,2,1,0:T(8,128)(2,1)S(1)}, u32[]{:S(2)}, u32[]{:S(2)}) async-start(bf16[16,1,160,384]{3,2,1,0:T(8,128)(2,1)} %broadcast_select_fusion), calls=%async_computation.1 | async-start | bytes 3932160 | tf_op jit(solution)/shard_map/all_to_all | solution.py:119
  97.9 3.0 copy-start.1
  111.2 5.0 %copy-start.5 = (s32[8]{0:T(128)S(1)}, s32[8]{0:T(128)}, u32[]{:S(2)}) copy-start(s32[8]{0:T(128)} %copy-done.4) | copy-start | bytes 100
  111.2 5.7 %copy-start.9 = (s32[8]{0:T(128)S(1)}, s32[8]{0:T(128)}, u32[]{:S(2)}) copy-start(s32[8]{0:T(128)} %copy-done.8) | copy-start | bytes 100
  111.2 6.4 %copy-start.7 = (s32[8]{0:T(128)S(1)}, s32[8]{0:T(128)}, u32[]{:S(2)}) copy-start(s32[8]{0:T(128)} %copy-done.6) | copy-start | bytes 100
  111.2 7.1 %copy-start.11 = (s32[1,8]{1,0:T(1,128)S(1)}, s32[1,8]{1,0:T(1,128)}, u32[]{:S(2)}) copy-start(s32[1,8]{1,0:T(1,128)} %copy-done.10) | copy-start | bytes 100
  111.2 7.1 %copy-start.13 = (s32[8,1]{0,1:T(1,128)S(1)}, s32[8,1]{0,1:T(1,128)}, u32[]{:S(2)}) copy-start(s32[8,1]{0,1:T(1,128)} %copy-done.12) | copy-start | bytes 100
  111.2 93.5 %all-to-all-start.2 = ((f32[16,1,160,384]{3,2,1,0:T(8,128)}), f32[16,1,160,384]{3,2,1,0:T(8,128)}, u32[]{:S(2)}, u32[]{:S(2)}) async-start(f32[16,1,160,384]{3,2,1,0:T(8,128)} %fusion.7), calls=%async_computation.2 | async-start | bytes 7864320 | tf_op jit(solution)/shard_map/all_to_all | solution.py:127
  116.0 145.5 %reduce-scatter.2.cloned.1.call-start = ((), (), s32[]{:S(2)}) async-start(), calls=%async_computation.4 | async-start | bytes 4587520 | tf_op jit(solution)/shard_map/reduce_scatter | solution.py:135
  211.8 2.1 copy-start.2
  213.8 1.0 copy-start.3
  217.7 73.6 %all-gather.2.cloned.1.call-start = ((), (), s32[]{:S(2)}) async-start(), calls=%async_computation.5 | async-start | bytes 1310720 | tf_op jit(solution)/shard_map/all_gather | solution.py:149
Sparse Core Ops, SparseCore 0:
  217.8 43.6 reduce-scatter.1
  263.6 27.6 all-gather.1
where the time goes:
time: 304 us; the launch traced here: 303 us
  waiting for transfers between devices  185 us (61%)
  local copies, waits for them, and re-layouts  24.7 us (8%)
  other arithmetic  23.1 us (8%)
  starting transfers between devices  20.6 us (7%)
  matrix products  19.9 us (7%)
  between operations  15 us (5%)
  blocking collectives  14.9 us (5%)
    all_to_all x1, waiting for transfers between devices, body(): lax.all_to_all(adapter_part, 'dp', split_axis=0, concat_axis=0, tiled=True)  71.2 us
    all_to_all x1, waiting for transfers between devices, body(): lax.all_to_all(outgoing, 'dp', split_axis=0, concat_axis=0, tiled=True)  45.2 us
    reduce_scatter x1, waiting for transfers between devices, body(): lax.psum_scatter(partial_value + jnp.concatenate([adapter_term, jnp.zeros...  43.7 us
    all_gather x1, waiting for transfers between devices, body(): lax.all_gather(kv_cache, 'col', axis=0, tiled=True)  25.1 us
    all_gather x1, blocking collectives, body(): gathered = lax.all_gather(hidden_states, 'row', axis=0, tiled=True)  14.9 us
    gather x2, other arithmetic, body(): starts[request_of]  10.9 us
    dot_general x1, matrix products, body(): jnp.einsum('nkla,af->nklf', reduced, flat_up, precision=lax.Precision.HIG...  10.3 us
    gather x2, local copies, waits for them, and re-layouts, body(): adapter_term = returned.reshape(-1, query_cols)[flat_index]  9.02 us
  transfers between devices with their start and end apart: 5, of which 4 were waited for; matrix products, arithmetic and copies ran while one was open for 10% of the time, Pallas kernels for 0%

commit v1 on v0

--- a/solution.py
+++ b/solution.py
@@ -1,3 +1,4 @@
+import functools
 import math
 import jax
 import jax.numpy as jnp
@@ -7,6 +8,27 @@
 HEAD_DIM = 128
 MOST_LEN = 160
 masked_score = -1e30
+
+
+def mark_flows(shard_in, named_axis):
+    fan = jax.lax.psum(1, named_axis)
+    piece_now = map(lambda dev_i: (dev_i, (dev_i + 1) % fan), range(fan))
+    rack = list(piece_now)
+    gallery = list(map(lambda dev_i: (dev_i, (dev_i - 1) % fan), range(fan)))
+    response, b_now = ([shard_in], [shard_in])
+    for _ in range(fan // 2):
+        spare = jax.lax.ppermute(response[-1], named_axis, rack)
+        response.append(spare)
+    for _ in range((fan - 1) // 2):
+        b_now.append(jax.lax.ppermute(b_now[-1], named_axis, gallery))
+    main = jnp.concatenate([*response[::-1], *b_now[1:]], axis=0)
+    all_values = jnp.roll(
+        main, (jax.lax.axis_index(named_axis) - fan // 2) * shard_in.shape[0], axis=0
+    )
+    return all_values
+
+
+table_press = functools.partial(mark_flows, named_axis="col")
 
 
 def block_layout(lengths_row, block_len):
@@ -145,9 +167,7 @@
     query_rows = summed[:, :query_cols].astype(jnp.bfloat16)
     kv_cache = summed[:, query_cols:].astype(jnp.bfloat16)
     attend, initial = make_attend(query_rows, segment, first_row, kv_group, head_size, kv_half)
-    running_max, running_sum, running_out = attend(
-        initial, lax.all_gather(kv_cache, "col", axis=0, tiled=True), jnp.int32(0)
-    )
+    running_max, running_sum, running_out = attend(initial, table_press(kv_cache), jnp.int32(0))
     attention = (running_out / running_sum[:, :, None]).astype(jnp.bfloat16)
     attention = jnp.transpose(attention, (1, 0, 2)).reshape(own_rows, query_cols)
     return (attention, kv_cache)

time: 304 us -> 293 us (0.964)
  waiting for transfers between devices: 185 us -> 173 us
  starting transfers between devices: 20.6 us -> 24.2 us
    all_gather x1 -> x0, waiting for transfers between devices: 25.1 us -> none  [body(): lax.all_gather(kv_cache, 'col', axis=0, tiled=True)]
    ppermute x0 -> x3, waiting for transfers between devices: none -> 12.3 us  [the longest x2 12.2 us: mark_flows(): spare = jax.lax.ppermute(response[-1], named_axis, rack)]
    ppermute x0 -> x3, starting transfers between devices: none -> 3.62 us  [the longest x1 3.31 us: mark_flows(): b_now.append(jax.lax.ppermute(b_now[-1], named_axis, gallery))]
  transfers between devices with their start and end apart: 5 -> 7, of which waited for: 4 -> 6; matrix products, arithmetic and copies ran while one was open for 10% -> 10% of each run, Pallas kernels for 0% -> 0%
where the time goes in v1:
time: 293 us; the launch traced here: 291 us
  waiting for transfers between devices  173 us (59%)
  starting transfers between devices  24.2 us (8%)
  local copies, waits for them, and re-layouts  23.3 us (8%)
  other arithmetic  23.1 us (8%)
  matrix products  18.2 us (6%)
  between operations  15 us (5%)
  blocking collectives  14.9 us (5%)
    all_to_all x1, waiting for transfers between devices, body(): lax.all_to_all(adapter_part, 'dp', split_axis=0, concat_axis=0, tiled=True)  71.2 us
    all_to_all x1, waiting for transfers between devices, body(): lax.all_to_all(outgoing, 'dp', split_axis=0, concat_axis=0, tiled=True)  45.2 us
    reduce_scatter x1, waiting for transfers between devices, body(): lax.psum_scatter(partial_value + jnp.concatenate([adapter_term, jnp.zeros...  43.8 us
    all_gather x1, blocking collectives, body(): gathered = lax.all_gather(hidden_states, 'row', axis=0, tiled=True)  14.9 us
    ppermute x2, waiting for transfers between devices, mark_flows(): spare = jax.lax.ppermute(response[-1], named_axis, rack)  12.2 us
    gather x2, other arithmetic, body(): starts[request_of]  10.9 us
    dot_general x1, matrix products, body(): jnp.einsum('nkla,af->nklf', reduced, flat_up, precision=lax.Precision.HIG...  10.3 us
    gather x2, local copies, waits for them, and re-layouts, body(): adapter_term = returned.reshape(-1, query_cols)[flat_index]  8.97 us
  transfers between devices with their start and end apart: 7, of which 6 were waited for; matrix products, arithmetic and copies ran while one was open for 10% of the time, Pallas kernels for 0%

profile of v1, /device:TPU:8, one launch (start us, length us, event | category | flops | bytes accessed | tf_op | source)
XLA Modules:
  0.0 291.3 jit_solution(123848767084259276)
XLA Ops:
  7.2 1.5 fusion.34
  11.0 0.7 copy.46
  11.7 8.6 %all-to-all-start = ((bf16[16,1,1]{2,1,0:T(2,128)(2,1)}), bf16[16,1,1]{2,1,0:T(2,128)(2,1)}, u32[]{:S(2)}, u32[]{:S(2)}) async-start(bf16[16,1,1]{2,1,0:T(2,128)(2,1)} %copy.46), calls=%async_computation | async-start | bytes 16384 | tf_op jit(solution)/shard_map/all_to_all | solution.py:142
  20.5 14.9 %all_gather.3 = bf16[1024,384]{1,0:T(8,128)(2,1)S(1)} all-gather(bf16[256,384]{1,0:T(8,128)(2,1)} %param.7), channel_id=1, replica_groups=mesh['row'=4,'col'=4,'dp'=16] {'row'}, dimensions={0}, use_global_device_ids=true | all-gather | bytes 983040 | tf_op jit(solution)/shard_map/all_gather | solution.py:94
  35.5 7.5 %gather_fusion = bf16[2560,384]{1,0:T(8,128)(2,1)S(1)} fusion(bf16[1024,384]{1,0:T(8,128)(2,1)S(1)} %all_gather.3, s32[3072]{0:T(1024)S(1)} %pad_clamp_fusion), kind=kCustom, calls=%fused_computation | custom fusion | bytes 3942400 | tf_op jit(solution)/shard_map/gather | solution.py:135
  43.0 1.5 broadcast_select_fusion
  44.5 7.0 %all-to-all-start.1 = ((bf16[16,1,160,384]{3,2,1,0:T(8,128)(2,1)}), bf16[16,1,160,384]{3,2,1,0:T(8,128)(2,1)S(1)}, u32[]{:S(2)}, u32[]{:S(2)}) async-start(bf16[16,1,160,384]{3,2,1,0:T(8,128)(2,1)} %broadcast_select_fusion), calls=%async_computation.1 | async-start | bytes 3932160 | tf_op jit(solution)/shard_map/all_to_all | solution.py:141
  51.5 1.1 convert_reduce_fusion.1
  52.7 45.2 %all-to-all-done.1 = bf16[16,1,160,384]{3,2,1,0:T(8,128)(2,1)S(1)} async-done(((bf16[16,1,160,384]{3,2,1,0:T(8,128)(2,1)}), bf16[16,1,160,384]{3,2,1,0:T(8,128)(2,1)S(1)}, u32[]{:S(2)}, u32[]{:S(2)}) %all-to-all-start.1) | async-done | bytes 1966112 | tf_op jit(solution)/shard_map/all_to_all | solution.py:141
  97.9 3.0 %fusion.10 = f32[16,160,1024]{2,1,0:T(8,128)S(1)} fusion(bf16[384,1024,1]{0,1,2:T(8,128)(2,1)S(1)} %bitcast.107, bf16[16,1,160,384]{3,2,1,0:T(8,128)(2,1)S(1)} %all-to-all-done.1), kind=kOutput, calls=%fused_computation.13 | convolution fusion | flops 2013265920 | bytes 13238272 | tf_op jit(solution)/shard_map/nkld,da->nkla/dot_general | solution.py:145
  100.9 10.3 %fusion.7 = f32[16,1,160,384]{3,2,1,0:T(8,128)} fusion(bf16[1024,384,1]{1,0,2:T(8,128)(2,1)S(1)} %bitcast.109, f32[16,160,1024]{2,1,0:T(8,128)S(1)} %fusion.10, pred[16,1024]{1,0:T(8,128)(4,1)S(1)} %broadcast_compare_fusion), kind=kOutput, calls=%fused_computation.12 | convolution fusion | flops 12082216960 | bytes 15220736 | tf_op jit(solution)/shard_map/nkla,af->nklf/dot_general | solution.py:148
  111.2 4.8 %all-to-all-start.2 = ((f32[16,1,160,384]{3,2,1,0:T(8,128)}), f32[16,1,160,384]{3,2,1,0:T(8,128)}, u32[]{:S(2)}, u32[]{:S(2)}) async-start(f32[16,1,160,384]{3,2,1,0:T(8,128)} %fusion.7), calls=%async_computation.2 | async-start | bytes 7864320 | tf_op jit(solution)/shard_map/all_to_all | solution.py:149
  116.2 0.7 fusion.50
  118.4 4.1 %select_select_fusion.2 = s32[1024,1]{0,1:T(1,128)S(1)} fusion(s32[]{:T(128)} %bitcast.20, s32[]{:T(128)} %bitcast.21, s32[]{:T(128)} %bitcast.22, s32[]{:T(128)} %bitcast.23, s32[]{:T(128)} %bitcast.24, s32[]{:T(128)} %bitcast.26, s32[]{:T(128)} %bitcast.25, s32[1024,1]{0,1:T(1,128)S(1)} %bitcast.113), kind=kLoop, calls=%fused_computation.64 | loop fusion | flops 15360 | bytes 8220 | tf_op jit(solution)/shard_map/gather | solution.py:150
  122.5 9.0 %select_select_fusion = (s32[1024,1]{0,1:T(1,128)S(1)}, s32[1024,1]{0,1:T(1,128)S(1)}) fusion(s32[]{:T(128)} %bitcast.39, s32[]{:T(128)} %bitcast.40, s32[]{:T(128)} %bitcast.41, s32[]{:T(128)} %bitcast.42, s32[]{:T(128)} %bitcast.43, s32[]{:T(128)} %bitcast.45, s32[]{:T(128)} %bitcast.44, s32[1024,1]{0,1:T(1,128)S(1)} %bitcast.114, s32[]{:T(128)} %bitcast.35, ...), kind=kLoop, calls=%fused_computation.62 | loop fusion | flops 21504 | bytes 12344 | tf_op jit(solution)/shard_map/gather | solution.py:151
  131.6 1.9 broadcast_select_fusion.2
  133.5 71.2 %all-to-all-done.2 = f32[16,1,160,384]{3,2,1,0:T(8,128)} async-done(((f32[16,1,160,384]{3,2,1,0:T(8,128)}), f32[16,1,160,384]{3,2,1,0:T(8,128)}, u32[]{:S(2)}, u32[]{:S(2)}) %all-to-all-start.2) | async-done | bytes 3932192 | tf_op jit(solution)/shard_map/all_to_all | solution.py:149
  204.7 7.1 %gather_fusion.1 = f32[1024,384]{1,0:T(8,128)} fusion(f32[2560,384]{1,0:T(8,128)} %bitcast.17, s32[1024]{0:T(1024)S(1)} %broadcast_clamp_fusion), kind=kCustom, calls=%fused_computation.1 | custom fusion | bytes 3149824 | tf_op jit(solution)/shard_map/gather | solution.py:153
  211.8 1.9 copy.50
  213.9 0.8 copy-done.2
  214.8 3.0 %bitcast_add_fusion = f32[1024,896]{0,1:T(8,128)} fusion(f32[1024,384]{0,1:T(8,128)S(1)} %broadcast_select_fusion.1, bf16[1024,384]{1,0:T(8,128)(2,1)S(1)} %all_gather.3, bf16[384,512]{1,0:T(8,128)(2,1)S(1)} %copy-done.2, bf16[384,384]{1,0:T(8,128)(2,1)S(1)} %copy-done.3), kind=kOutput, calls=%fused_computation.6 | convolution fusion | flops 706936832 | bytes 6717440 | tf_op jit(solution)/shard_map/dot_general | solution.py:156
  217.8 43.8 %reduce-scatter.2.cloned.1.call-done = f32[256,896]{0,1:T(8,128)} async-done(((f32[1024,896]{0,1:T(8,128)}), f32[256,896]{0,1:T(8,128)}) %reduce-scatter.2.cloned.1.call-update) | async-done | bytes 917520 | tf_op jit(solution)/shard_map/reduce_scatter | solution.py:157
  261.6 1.2 convert.5
  263.1 9.0 %collective-permute-done = bf16[256,512]{0,1:T(8,128)(2,1)S(1)} collective-permute-done((bf16[256,512]{0,1:T(8,128)(2,1)S(1)}, bf16[256,512]{0,1:T(8,128)(2,1)S(1)}, u32[]{:S(2)}, u32[]{:S(2)}) %collective-permute-start) | collective-permute-done | bytes 262176 | tf_op jit(solution)/shard_map/ppermute | solution.py:20
  272.2 0.8 fusion.18
  273.0 3.3 %collective-permute-start.2 = (bf16[256,512]{0,1:T(8,128)(2,1)S(1)}, bf16[256,512]{0,1:T(8,128)(2,1)S(1)}, u32[]{:S(2)}, u32[]{:S(2)}) collective-permute-start(bf16[256,512]{0,1:T(8,128)(2,1)S(1)} %slice.41), channel_id=1, source_target_pairs={{0,48},{16,0},{32,16},{48,32},{1,49},{17,1},{33,17},{49,33},{2,50}... | collective-permute-start | bytes 786440 | tf_op jit(solution)/shard_map/ppermute | solution.py:23
  276.3 0.8 copy.55
  277.1 3.3 %collective-permute-done.1 = bf16[256,512]{0,1:T(8,128)(2,1)S(1)} collective-permute-done((bf16[256,512]{0,1:T(8,128)(2,1)S(1)}, bf16[256,512]{0,1:T(8,128)(2,1)S(1)}, u32[]{:S(2)}, u32[]{:S(2)}) %collective-permute-start.1) | collective-permute-done | bytes 262176 | tf_op jit(solution)/shard_map/ppermute | solution.py:20
  280.8 0.9 fusion.4
  281.7 0.8 fusion.5
  282.5 1.1 fusion.22
  283.6 0.8 copy.54
  (71 shorter events, 4.8 us)
Async XLA Ops:
  7.2 90.7 %copy-start = (bf16[64,384,16]{1,2,0:T(8,128)(2,1)S(1)}, bf16[64,384,16]{1,2,0:T(8,128)(2,1)}, u32[]{:S(2)}) copy-start(bf16[64,384,16]{1,2,0:T(8,128)(2,1)} %param.10) | copy-start | bytes 2359300
  8.8 11.6 %copy-start.10 = (s32[1,8]{1,0:T(1,128)}, s32[1,8]{1,0:T(1,128)S(1)}, u32[]{:S(2)}) copy-start(s32[1,8]{1,0:T(1,128)S(1)} %copy.62) | copy-start | bytes 100
  8.9 11.4 %copy-start.12 = (s32[8,1]{0,1:T(1,128)}, s32[8,1]{0,1:T(1,128)S(1)}, u32[]{:S(2)}) copy-start(s32[8,1]{0,1:T(1,128)S(1)} %reduce-window.4) | copy-start | bytes 100
  9.0 11.4 %copy-start.6 = (s32[8]{0:T(128)}, s32[8]{0:T(128)S(1)}, u32[]{:S(2)}) copy-start(s32[8]{0:T(128)S(1)} %get-tuple-element.49) | copy-start | bytes 100
  9.1 0.5 copy-start.8
  10.4 0.5 copy-start.4
  11.7 32.8 %all-to-all-start = ((bf16[16,1,1]{2,1,0:T(2,128)(2,1)}), bf16[16,1,1]{2,1,0:T(2,128)(2,1)}, u32[]{:S(2)}, u32[]{:S(2)}) async-start(bf16[16,1,1]{2,1,0:T(2,128)(2,1)} %copy.46), calls=%async_computation | async-start | bytes 16384 | tf_op jit(solution)/shard_map/all_to_all | solution.py:142
  44.5 53.4 %all-to-all-start.1 = ((bf16[16,1,160,384]{3,2,1,0:T(8,128)(2,1)}), bf16[16,1,160,384]{3,2,1,0:T(8,128)(2,1)S(1)}, u32[]{:S(2)}, u32[]{:S(2)}) async-start(bf16[16,1,160,384]{3,2,1,0:T(8,128)(2,1)} %broadcast_select_fusion), calls=%async_computation.1 | async-start | bytes 3932160 | tf_op jit(solution)/shard_map/all_to_all | solution.py:141
  97.9 3.0 %copy-start.1 = (bf16[64,16,384]{2,1,0:T(8,128)(2,1)S(1)}, bf16[64,16,384]{2,1,0:T(8,128)(2,1)}, u32[]{:S(2)}) copy-start(bf16[64,16,384]{2,1,0:T(8,128)(2,1)} %param.11) | copy-start | bytes 2359300
  111.2 5.0 %copy-start.5 = (s32[8]{0:T(128)S(1)}, s32[8]{0:T(128)}, u32[]{:S(2)}) copy-start(s32[8]{0:T(128)} %copy-done.4) | copy-start | bytes 100
  111.2 5.7 %copy-start.9 = (s32[8]{0:T(128)S(1)}, s32[8]{0:T(128)}, u32[]{:S(2)}) copy-start(s32[8]{0:T(128)} %copy-done.8) | copy-start | bytes 100
  111.2 6.4 %copy-start.7 = (s32[8]{0:T(128)S(1)}, s32[8]{0:T(128)}, u32[]{:S(2)}) copy-start(s32[8]{0:T(128)} %copy-done.6) | copy-start | bytes 100
  111.2 7.1 %copy-start.11 = (s32[1,8]{1,0:T(1,128)S(1)}, s32[1,8]{1,0:T(1,128)}, u32[]{:S(2)}) copy-start(s32[1,8]{1,0:T(1,128)} %copy-done.10) | copy-start | bytes 100
  111.2 7.1 %copy-start.13 = (s32[8,1]{0,1:T(1,128)S(1)}, s32[8,1]{0,1:T(1,128)}, u32[]{:S(2)}) copy-start(s32[8,1]{0,1:T(1,128)} %copy-done.12) | copy-start | bytes 100
  111.2 93.5 %all-to-all-start.2 = ((f32[16,1,160,384]{3,2,1,0:T(8,128)}), f32[16,1,160,384]{3,2,1,0:T(8,128)}, u32[]{:S(2)}, u32[]{:S(2)}) async-start(f32[16,1,160,384]{3,2,1,0:T(8,128)} %fusion.7), calls=%async_computation.2 | async-start | bytes 7864320 | tf_op jit(solution)/shard_map/all_to_all | solution.py:149
  116.0 145.6 %reduce-scatter.2.cloned.1.call-start = ((), (), s32[]{:S(2)}) async-start(), calls=%async_computation.4 | async-start | bytes 4587520 | tf_op jit(solution)/shard_map/reduce_scatter | solution.py:157
  213.7 1.0 copy-start.2
  213.7 1.1 copy-start.3
  262.8 9.3 %collective-permute-start = (bf16[256,512]{0,1:T(8,128)(2,1)S(1)}, bf16[256,512]{0,1:T(8,128)(2,1)S(1)}, u32[]{:S(2)}, u32[]{:S(2)}) collective-permute-start(bf16[256,512]{0,1:T(8,128)(2,1)S(1)} %slice.41), channel_id=1, source_target_pairs={{0,16},{16,32},{32,48},{48,0},{1,17},{17,33},{33,49},{49,1},{2,18}... | collective-permute-start | bytes 786440 | tf_op jit(solution)/shard_map/ppermute | solution.py:20
  272.1 8.3 %collective-permute-start.1 = (bf16[256,512]{0,1:T(8,128)(2,1)S(1)}, bf16[256,512]{0,1:T(8,128)(2,1)S(1)}, u32[]{:S(2)}, u32[]{:S(2)}) collective-permute-start(bf16[256,512]{0,1:T(8,128)(2,1)S(1)} %collective-permute-done), channel_id=1, source_target_pairs={{0,16},{16,32},{32,48},{48,0},{1,17},{17,33},{33,49},{49,1},{2,18}... | collective-permute-start | bytes 786440 | tf_op jit(solution)/shard_map/ppermute | solution.py:20
  273.0 7.7 %collective-permute-start.2 = (bf16[256,512]{0,1:T(8,128)(2,1)S(1)}, bf16[256,512]{0,1:T(8,128)(2,1)S(1)}, u32[]{:S(2)}, u32[]{:S(2)}) collective-permute-start(bf16[256,512]{0,1:T(8,128)(2,1)S(1)} %slice.41), channel_id=1, source_target_pairs={{0,48},{16,0},{32,16},{48,32},{1,49},{17,1},{33,17},{49,33},{2,50}... | collective-permute-start | bytes 786440 | tf_op jit(solution)/shard_map/ppermute | solution.py:23
Sparse Core Ops, SparseCore 0:
  217.9 43.6 reduce-scatter.1
